TPU v7x, 256 devices: a whole 4x4x8 slice. The times are simulated.
256 devices in a mesh: node: 32 (over y, x, z_lo), shot: 8 (over z_hi, core).
Axes of the slice: x: 4, y: 4, z: 8 (z_hi: 4, z_lo: 2; z = z_hi * 2 + z_lo), core: 2. Of those that a mesh axis runs over, the one named last changes fastest.
Arguments:
- spectra: bfloat16 [64, 2, 1024, 4096], P(None, None, 'shot', 'node'), may hold values from -6 to 6
- source_block: int32 [6], replicated, may hold values from 0 to 127
- taper_window: int32 [6, 1024], replicated, may hold values from 0 to 7
Outputs:
- virtual_gathers: bfloat16 [6, 64, 2, 32, 4096], P(None, 'shot', None, None, 'node')
All inputs are finite; a program needn't handle non-finite values.
Results may differ from a plain program's by a relative error of at most 0.0047.
Values may be sent and summed in bfloat16 or wider, within the bound.
No kernel may reach another device: no remote copies, remote signals or barrier semaphores. Data moves between devices by JAX's collectives and lax.ppermute only.
A program may use at most 128 MiB of HBM per device.

v0:
```python
import jax
import jax.numpy as jnp
import numpy as np
from jax import lax
from jax.sharding import Mesh, PartitionSpec as P

SB = 32
ROUNDS = 6
WINDOWS = 8
CHUNKS = 2
PLANE = ("y", "x")


def taper_weights(taper_windows):
    return 0.5 - 0.5 * jnp.cos(jnp.pi * (taper_windows.astype(jnp.float32) + 1.0) / (WINDOWS + 1.0))


def pick_sources(spectra, source_block):
    node_dev = spectra.shape[3]
    per_device = node_dev // SB
    me = (lax.axis_index("y") * lax.axis_size("x") + lax.axis_index("x")) * lax.axis_size(
        "zl"
    ) + lax.axis_index("zl")
    owner = source_block // per_device
    first = source_block % per_device * SB
    column = jnp.arange(ROUNDS * SB, dtype=jnp.int32)
    wanted = first[column // SB] + column % SB
    keep = owner[column // SB] == me
    node = jnp.arange(node_dev, dtype=jnp.int32)
    select = ((node[:, None] == wanted[None, :]) & keep[None, :]).astype(spectra.dtype)
    select = select.reshape(node_dev, CHUNKS, ROUNDS * SB // CHUNKS)
    picked = jnp.einsum("fckn,nhq->hfcqk", spectra, select, preferred_element_type=jnp.float32)
    return picked.astype(spectra.dtype)


def broadcast(piece, pending=None):
    part = lax.psum_scatter(piece, PLANE, scatter_dimension=0, tiled=True)
    other = lax.ppermute(part, "zl", perm=[(0, 1), (1, 0)])
    part = part + other
    if pending is not None:
        part, pending = lax.optimization_barrier((part, pending))
    return (lax.all_gather(part, PLANE, axis=0, tiled=True), pending)


def shot_reduce(partial):
    nz = lax.axis_size("zh")
    nc = lax.axis_size("c")
    zh = lax.axis_index("zh")
    c = lax.axis_index("c")
    freqs = partial.shape[0]
    grouped = partial.reshape(nz, nc, freqs // (nz * nc), *partial.shape[1:])
    send = lax.dynamic_index_in_dim(grouped, 1 - c, axis=1, keepdims=False)
    keep = lax.dynamic_index_in_dim(grouped, c, axis=1, keepdims=False)
    mine = keep + lax.ppermute(send, "c", perm=[(0, 1), (1, 0)])
    half = mine.shape[-1] // 2
    forward = mine[..., :half]
    backward = mine[..., half:]
    up = [(j, (j + 1) % nz) for j in range(nz)]
    down = [(j, (j - 1) % nz) for j in range(nz)]
    acc_f = lax.dynamic_index_in_dim(forward, (zh - 1) % nz, axis=0, keepdims=False)
    acc_b = lax.dynamic_index_in_dim(backward, (zh + 1) % nz, axis=0, keepdims=False)
    for step in range(nz - 1):
        got_f = lax.ppermute(acc_f, "zh", perm=up)
        got_b = lax.ppermute(acc_b, "zh", perm=down)
        acc_f = got_f + lax.dynamic_index_in_dim(
            forward, (zh - 2 - step) % nz, axis=0, keepdims=False
        )
        acc_b = got_b + lax.dynamic_index_in_dim(
            backward, (zh + 2 + step) % nz, axis=0, keepdims=False
        )
    return jnp.concatenate((acc_f, acc_b), axis=-1)


def body(spectra, source_block, taper_window):
    freqs, _, shot_dev, node_dev = spectra.shape
    shot_groups = lax.axis_size("zh") * lax.axis_size("c")
    scale = 1.0 / jnp.sqrt(jnp.float32(shot_dev * shot_groups))
    shot_weights = taper_weights(taper_window)
    shot_index = lax.axis_index("zh") * lax.axis_size("c") + lax.axis_index("c")
    local_weights = lax.dynamic_slice_in_dim(shot_weights, shot_index * shot_dev, shot_dev, 1)
    weight_rows = jnp.repeat(local_weights, SB, axis=0).reshape(CHUNKS, -1, shot_dev)
    receivers = spectra.reshape(freqs, 2 * shot_dev, node_dev)
    picked = pick_sources(spectra, source_block)
    results = []
    summed = None
    for chunk in range(CHUNKS):
        piece = picked[chunk]
        pending = None
        if summed is not None:
            piece, summed = lax.optimization_barrier((piece, summed))
            pending = shot_reduce(summed * scale)
        source, pending = broadcast(piece, pending)
        if pending is not None:
            results.append(pending)
        tapered = (source.astype(jnp.float32) * weight_rows[chunk][None, None]).astype(jnp.bfloat16)
        real_part = tapered[:, 0]
        imag_part = tapered[:, 1]
        real_row = jnp.concatenate((real_part, imag_part), axis=2)
        imag_row = jnp.concatenate((-imag_part, real_part), axis=2)
        operator = jnp.stack((real_row, imag_row), axis=1)
        summed = jnp.einsum(
            "foqK,fKn->foqn", operator, receivers, preferred_element_type=jnp.float32
        )
    results.append(shot_reduce(summed * scale))
    reduced = jnp.concatenate(results, axis=2)
    local_f = reduced.shape[0]
    reduced = reduced.reshape(local_f, 2, ROUNDS, SB, node_dev)
    return jnp.transpose(reduced, (2, 0, 1, 3, 4)).astype(jnp.bfloat16)


def solution(mesh):
    devices = np.asarray(mesh.devices).reshape(4, 4, 2, 4, 2)
    fine = Mesh(devices, ("y", "x", "zl", "zh", "c"))
    in_specs = (P(None, None, ("zh", "c"), ("y", "x", "zl")), P(), P())
    out_specs = P(None, ("zh", "c"), None, None, ("y", "x", "zl"))
    return jax.shard_map(body, mesh=fine, in_specs=in_specs, out_specs=out_specs, check_vma=False)
```

profile of v0, /device:TPU:1, one launch (start us, length us, event | category | flops | bytes accessed | tf_op | source)
XLA Modules:
  0.0 471.3 jit_solution(1348825625948598850)
XLA Ops:
  7.9 3.7 fusion.28
  11.7 3.8 compare_reduce_fusion
  15.6 4.0 convert_bitcast_fusion
  19.6 3.9 slice_bitcast_fusion
  23.5 82.9 %reduce-scatter.3.cloned.1.call-done = bf16[4,2,96,128]{3,2,1,0:T(8,128)(2,1)} async-done(((bf16[64,2,96,128]{3,2,1,0:T(8,128)(2,1)}), bf16[4,2,96,128]{3,2,1,0:T(8,128)(2,1)}) %reduce-scatter.3.cloned.1.call-update) | async-done | bytes 196624 | tf_op jit(solution)/shard_map/reduce_scatter | solution.py:37
  107.8 3.4 collective-permute-done
  113.7 54.2 %all-gather.3.cloned.1.call-done = bf16[64,2,96,128]{3,2,1,0:T(8,128)(2,1)} async-done(((bf16[4,2,96,128]{3,2,1,0:T(8,128)(2,1)}), bf16[64,2,96,128]{3,2,1,0:T(8,128)(2,1)}) %all-gather.3.cloned.1.call-update) | async-done | bytes 3145744 | tf_op jit(solution)/shard_map/all_gather | solution.py:42
  167.9 2.5 multiply_convert_fusion.1
  173.0 3.6 fusion
  176.6 3.4 broadcast_multiply_fusion.1
  183.8 5.3 %collective-permute-done.2 = f32[4,8,2,96,128]{4,3,2,1,0:T(8,128)} collective-permute-done((f32[4,8,2,96,128]{4,3,2,1,0:T(8,128)S(1)}, f32[4,8,2,96,128]{4,3,2,1,0:T(8,128)}, u32[]{:S(2)}, u32[]{:S(2)}) %collective-permute-start.2) | collective-permute-done | bytes 3145760 | tf_op jit(solution)/shard_map/ppermute | solution.py:54
  189.1 3.4 bitcast_add_fusion.1
  199.0 3.8 collective-permute-start.6
  210.9 20.5 %collective-permute-done.6 = f32[8,2,96,64]{2,3,1,0:T(8,128)} collective-permute-done((f32[8,2,96,64]{2,3,1,0:T(8,128)}, f32[8,2,96,64]{2,3,1,0:T(8,128)}, u32[]{:S(2)}, u32[]{:S(2)}) %collective-permute-start.6) | collective-permute-done | bytes 393248 | tf_op jit(solution)/shard_map/ppermute | solution.py:64
  233.5 4.5 collective-permute-start.7
  244.4 6.8 %collective-permute-done.7 = f32[8,2,96,64]{2,3,1,0:T(8,128)} collective-permute-done((f32[8,2,96,64]{2,3,1,0:T(8,128)}, f32[8,2,96,64]{2,3,1,0:T(8,128)}, u32[]{:S(2)}, u32[]{:S(2)}) %collective-permute-start.7) | collective-permute-done | bytes 393248 | tf_op jit(solution)/shard_map/ppermute | solution.py:64
  253.3 2.7 collective-permute-start.8
  256.0 5.8 %collective-permute-done.4 = f32[8,2,96,64]{2,3,1,0:T(8,128)} collective-permute-done((f32[8,2,96,64]{2,3,1,0:T(8,128)}, f32[8,2,96,64]{2,3,1,0:T(8,128)}, u32[]{:S(2)}, u32[]{:S(2)}) %collective-permute-start.4) | collective-permute-done | bytes 393248 | tf_op jit(solution)/shard_map/ppermute | solution.py:63
  266.0 9.4 %collective-permute-done.8 = f32[8,2,96,64]{2,3,1,0:T(8,128)} collective-permute-done((f32[8,2,96,64]{2,3,1,0:T(8,128)}, f32[8,2,96,64]{2,3,1,0:T(8,128)}, u32[]{:S(2)}, u32[]{:S(2)}) %collective-permute-start.8) | collective-permute-done | bytes 393248 | tf_op jit(solution)/shard_map/ppermute | solution.py:64
  277.6 7.9 %collective-permute-done.5 = f32[8,2,96,64]{2,3,1,0:T(8,128)} collective-permute-done((f32[8,2,96,64]{2,3,1,0:T(8,128)}, f32[8,2,96,64]{2,3,1,0:T(8,128)}, u32[]{:S(2)}, u32[]{:S(2)}) %collective-permute-start.5) | collective-permute-done | bytes 393248 | tf_op jit(solution)/shard_map/ppermute | solution.py:63
  291.5 2.5 collective-permute-done.1
  294.7 55.8 %all-gather.5.cloned.1.call-done = bf16[64,2,96,128]{3,2,1,0:T(8,128)(2,1)} async-done(((bf16[4,2,96,128]{3,2,1,0:T(8,128)(2,1)}), bf16[64,2,96,128]{3,2,1,0:T(8,128)(2,1)}) %all-gather.5.cloned.1.call-update) | async-done | bytes 3145744 | tf_op jit(solution)/shard_map/all_gather | solution.py:42
  350.5 2.5 multiply_convert_fusion
  358.9 5.3 %collective-permute-done.9 = f32[4,8,2,96,128]{4,3,2,1,0:T(8,128)S(1)} collective-permute-done((f32[4,8,2,96,128]{4,3,2,1,0:T(8,128)S(1)}, f32[4,8,2,96,128]{4,3,2,1,0:T(8,128)S(1)}, u32[]{:S(2)}, u32[]{:S(2)}) %collective-permute-start.9) | collective-permute-done | bytes 3145760 | tf_op jit(solution)/shard_map/ppermute | solution.py:54
  371.2 3.8 collective-permute-start.13
  380.9 22.7 %collective-permute-done.13 = f32[8,2,96,64]{2,3,1,0:T(8,128)} collective-permute-done((f32[8,2,96,64]{2,3,1,0:T(8,128)}, f32[8,2,96,64]{2,3,1,0:T(8,128)}, u32[]{:S(2)}, u32[]{:S(2)}) %collective-permute-start.13) | collective-permute-done | bytes 393248 | tf_op jit(solution)/shard_map/ppermute | solution.py:64
  405.7 4.5 collective-permute-start.14
  418.9 4.6 collective-permute-done.14
  424.7 2.8 collective-permute-start.15
  427.5 6.6 %collective-permute-done.11 = f32[8,2,96,64]{2,3,1,0:T(8,128)} collective-permute-done((f32[8,2,96,64]{2,3,1,0:T(8,128)}, f32[8,2,96,64]{2,3,1,0:T(8,128)}, u32[]{:S(2)}, u32[]{:S(2)}) %collective-permute-start.11) | collective-permute-done | bytes 393248 | tf_op jit(solution)/shard_map/ppermute | solution.py:63
  438.2 9.4 %collective-permute-done.15 = f32[8,2,96,64]{2,3,1,0:T(8,128)} collective-permute-done((f32[8,2,96,64]{2,3,1,0:T(8,128)S(1)}, f32[8,2,96,64]{2,3,1,0:T(8,128)}, u32[]{:S(2)}, u32[]{:S(2)}) %collective-permute-start.15) | collective-permute-done | bytes 393248 | tf_op jit(solution)/shard_map/ppermute | solution.py:64
  452.0 7.0 %collective-permute-done.12 = f32[8,2,96,64]{2,3,1,0:T(8,128)} collective-permute-done((f32[8,2,96,64]{2,3,1,0:T(8,128)}, f32[8,2,96,64]{2,3,1,0:T(8,128)}, u32[]{:S(2)}, u32[]{:S(2)}) %collective-permute-start.12) | collective-permute-done | bytes 393248 | tf_op jit(solution)/shard_map/ppermute | solution.py:63
  (93 shorter events, 94.9 us)
Async XLA Ops:
  6.5 99.9 %reduce-scatter.3.cloned.1.call-start = ((), (), s32[]{:S(2)}) async-start(), calls=%async_computation.2 | async-start | bytes 3342336 | tf_op jit(solution)/shard_map/reduce_scatter | solution.py:37
  23.5 144.4 %all-gather.3.cloned.1.call-start = ((), (), s32[]{:S(2)}) async-start(), calls=%async_computation.3 | async-start | bytes 3342336 | tf_op jit(solution)/shard_map/all_gather | solution.py:42
  106.5 4.7 %collective-permute-start = (bf16[4,2,96,128]{3,2,1,0:T(8,128)(2,1)}, bf16[4,2,96,128]{3,2,1,0:T(8,128)(2,1)S(1)}, u32[]{:S(2)}, u32[]{:S(2)}) collective-permute-start(bf16[4,2,96,128]{3,2,1,0:T(8,128)(2,1)} %reduce-scatter.3.cloned.1.call-done), channel_id=1, source_target_pairs={{0,8},{8,0},{1,9},{9,1},{2,10},{10,2},{3,11},{11,3},{4,12},{12,4},... | collective-permute-start | bytes 589832 | tf_op jit(solution)/shard_map/ppermute | solution.py:38
  112.9 176.2 %reduce-scatter.5.cloned.1.call-start = ((), (), s32[]{:S(2)}) async-start(), calls=%async_computation.4 | async-start | bytes 3342336 | tf_op jit(solution)/shard_map/reduce_scatter | solution.py:37
  170.8 2.2 copy-start.3
  180.1 2.6 copy-start
  182.7 6.4 %collective-permute-start.2 = (f32[4,8,2,96,128]{4,3,2,1,0:T(8,128)S(1)}, f32[4,8,2,96,128]{4,3,2,1,0:T(8,128)}, u32[]{:S(2)}, u32[]{:S(2)}) collective-permute-start(f32[4,8,2,96,128]{4,3,2,1,0:T(8,128)S(1)} %dynamic-slice_bitcast_fusion.1), channel_id=1, source_target_pairs={{0,1},{1,0},{2,3},{3,2},{4,5},{5,4},{6,7},{7,6},{8,9},{9,8},{10,11... | collective-permute-start | bytes 9437192 | tf_op jit(solution)/shard_map/ppermute | solution.py:54
  183.7 166.8 %all-gather.5.cloned.1.call-start = ((), (), s32[]{:S(2)}) async-start(), calls=%async_computation.5 | async-start | bytes 3342336 | tf_op jit(solution)/shard_map/all_gather | solution.py:42
  193.7 1.6 copy-start.1
  199.0 32.4 %collective-permute-start.6 = (f32[8,2,96,64]{2,3,1,0:T(8,128)}, f32[8,2,96,64]{2,3,1,0:T(8,128)}, u32[]{:S(2)}, u32[]{:S(2)}) collective-permute-start(f32[8,2,96,64]{2,3,1,0:T(8,128)} %bitcast.113), channel_id=1, source_target_pairs={{0,6},{2,0},{4,2},{6,4},{1,7},{3,1},{5,3},{7,5},{8,14},{10,8},{12,... | collective-permute-start | bytes 1179656 | tf_op jit(solution)/shard_map/ppermute | solution.py:64
  206.5 31.4 %collective-permute-start.3 = (f32[8,2,96,64]{2,3,1,0:T(8,128)}, f32[8,2,96,64]{2,3,1,0:T(8,128)}, u32[]{:S(2)}, u32[]{:S(2)}) collective-permute-start(f32[8,2,96,64]{2,3,1,0:T(8,128)} %bitcast.115), channel_id=1, source_target_pairs={{0,2},{2,4},{4,6},{6,0},{1,3},{3,5},{5,7},{7,1},{8,10},{10,12},{12... | collective-permute-start | bytes 1179656 | tf_op jit(solution)/shard_map/ppermute | solution.py:63
  233.5 17.8 %collective-permute-start.7 = (f32[8,2,96,64]{2,3,1,0:T(8,128)}, f32[8,2,96,64]{2,3,1,0:T(8,128)}, u32[]{:S(2)}, u32[]{:S(2)}) collective-permute-start(f32[8,2,96,64]{2,3,1,0:T(8,128)} %bitcast_add_fusion.11), channel_id=1, source_target_pairs={{0,6},{2,0},{4,2},{6,4},{1,7},{3,1},{5,3},{7,5},{8,14},{10,8},{12,... | collective-permute-start | bytes 1179656 | tf_op jit(solution)/shard_map/ppermute | solution.py:64
  240.0 21.8 %collective-permute-start.4 = (f32[8,2,96,64]{2,3,1,0:T(8,128)}, f32[8,2,96,64]{2,3,1,0:T(8,128)}, u32[]{:S(2)}, u32[]{:S(2)}) collective-permute-start(f32[8,2,96,64]{2,3,1,0:T(8,128)} %bitcast_add_fusion.13), channel_id=1, source_target_pairs={{0,2},{2,4},{4,6},{6,0},{1,3},{3,5},{5,7},{7,1},{8,10},{10,12},{12... | collective-permute-start | bytes 1179656 | tf_op jit(solution)/shard_map/ppermute | solution.py:63
  253.3 22.1 %collective-permute-start.8 = (f32[8,2,96,64]{2,3,1,0:T(8,128)}, f32[8,2,96,64]{2,3,1,0:T(8,128)}, u32[]{:S(2)}, u32[]{:S(2)}) collective-permute-start(f32[8,2,96,64]{2,3,1,0:T(8,128)} %bitcast_add_fusion.10), channel_id=1, source_target_pairs={{0,6},{2,0},{4,2},{6,4},{1,7},{3,1},{5,3},{7,5},{8,14},{10,8},{12,... | collective-permute-start | bytes 1179656 | tf_op jit(solution)/shard_map/ppermute | solution.py:64
  263.9 21.6 %collective-permute-start.5 = (f32[8,2,96,64]{2,3,1,0:T(8,128)}, f32[8,2,96,64]{2,3,1,0:T(8,128)}, u32[]{:S(2)}, u32[]{:S(2)}) collective-permute-start(f32[8,2,96,64]{2,3,1,0:T(8,128)} %bitcast_add_fusion.12), channel_id=1, source_target_pairs={{0,2},{2,4},{4,6},{6,0},{1,3},{3,5},{5,7},{7,1},{8,10},{10,12},{12... | collective-permute-start | bytes 1179656 | tf_op jit(solution)/shard_map/ppermute | solution.py:63
  289.1 4.8 %copy-start.6 = (bf16[4,2,96,128]{3,2,1,0:T(8,128)(2,1)S(1)}, bf16[4,2,96,128]{3,2,1,0:T(8,128)(2,1)}, u32[]{:S(2)}) copy-start(bf16[4,2,96,128]{3,2,1,0:T(8,128)(2,1)} %reduce-scatter.5.cloned.1.call-done) | copy-start | bytes 589828
  289.2 4.8 %collective-permute-start.1 = (bf16[4,2,96,128]{3,2,1,0:T(8,128)(2,1)}, bf16[4,2,96,128]{3,2,1,0:T(8,128)(2,1)S(1)}, u32[]{:S(2)}, u32[]{:S(2)}) collective-permute-start(bf16[4,2,96,128]{3,2,1,0:T(8,128)(2,1)} %reduce-scatter.5.cloned.1.call-done), channel_id=1, source_target_pairs={{0,8},{8,0},{1,9},{9,1},{2,10},{10,2},{3,11},{11,3},{4,12},{12,4},... | collective-permute-start | bytes 589832 | tf_op jit(solution)/shard_map/ppermute | solution.py:38
  353.4 2.2 copy-start.4
  357.8 6.4 %collective-permute-start.9 = (f32[4,8,2,96,128]{4,3,2,1,0:T(8,128)S(1)}, f32[4,8,2,96,128]{4,3,2,1,0:T(8,128)S(1)}, u32[]{:S(2)}, u32[]{:S(2)}) collective-permute-start(f32[4,8,2,96,128]{4,3,2,1,0:T(8,128)S(1)} %dynamic-slice_bitcast_fusion), channel_id=1, source_target_pairs={{0,1},{1,0},{2,3},{3,2},{4,5},{5,4},{6,7},{7,6},{8,9},{9,8},{10,11... | collective-permute-start | bytes 9437192 | tf_op jit(solution)/shard_map/ppermute | solution.py:54
  365.9 1.6 copy-start.2
  371.2 32.4 %collective-permute-start.13 = (f32[8,2,96,64]{2,3,1,0:T(8,128)}, f32[8,2,96,64]{2,3,1,0:T(8,128)}, u32[]{:S(2)}, u32[]{:S(2)}) collective-permute-start(f32[8,2,96,64]{2,3,1,0:T(8,128)} %bitcast.114), channel_id=1, source_target_pairs={{0,6},{2,0},{4,2},{6,4},{1,7},{3,1},{5,3},{7,5},{8,14},{10,8},{12,... | collective-permute-start | bytes 1179656 | tf_op jit(solution)/shard_map/ppermute | solution.py:64
  378.7 33.8 %collective-permute-start.10 = (f32[8,2,96,64]{2,3,1,0:T(8,128)}, f32[8,2,96,64]{2,3,1,0:T(8,128)}, u32[]{:S(2)}, u32[]{:S(2)}) collective-permute-start(f32[8,2,96,64]{2,3,1,0:T(8,128)} %bitcast.116), channel_id=1, source_target_pairs={{0,2},{2,4},{4,6},{6,0},{1,3},{3,5},{5,7},{7,1},{8,10},{10,12},{12... | collective-permute-start | bytes 1179656 | tf_op jit(solution)/shard_map/ppermute | solution.py:63
  405.7 17.7 %collective-permute-start.14 = (f32[8,2,96,64]{2,3,1,0:T(8,128)}, f32[8,2,96,64]{2,3,1,0:T(8,128)}, u32[]{:S(2)}, u32[]{:S(2)}) collective-permute-start(f32[8,2,96,64]{2,3,1,0:T(8,128)} %bitcast_add_fusion.7), channel_id=1, source_target_pairs={{0,6},{2,0},{4,2},{6,4},{1,7},{3,1},{5,3},{7,5},{8,14},{10,8},{12,... | collective-permute-start | bytes 1179656 | tf_op jit(solution)/shard_map/ppermute | solution.py:64
  414.5 19.5 %collective-permute-start.11 = (f32[8,2,96,64]{2,3,1,0:T(8,128)}, f32[8,2,96,64]{2,3,1,0:T(8,128)}, u32[]{:S(2)}, u32[]{:S(2)}) collective-permute-start(f32[8,2,96,64]{2,3,1,0:T(8,128)} %bitcast_add_fusion.9), channel_id=1, source_target_pairs={{0,2},{2,4},{4,6},{6,0},{1,3},{3,5},{5,7},{7,1},{8,10},{10,12},{12... | collective-permute-start | bytes 1179656 | tf_op jit(solution)/shard_map/ppermute | solution.py:63
  424.7 22.9 %collective-permute-start.15 = (f32[8,2,96,64]{2,3,1,0:T(8,128)S(1)}, f32[8,2,96,64]{2,3,1,0:T(8,128)}, u32[]{:S(2)}, u32[]{:S(2)}) collective-permute-start(f32[8,2,96,64]{2,3,1,0:T(8,128)S(1)} %bitcast_add_fusion.6), channel_id=1, source_target_pairs={{0,6},{2,0},{4,2},{6,4},{1,7},{3,1},{5,3},{7,5},{8,14},{10,8},{12,... | collective-permute-start | bytes 1179656 | tf_op jit(solution)/shard_map/ppermute | solution.py:64
  436.1 26.4 %copy-start.5 = (bf16[8,2,96,128]{3,2,1,0:T(8,128)(2,1)S(1)}, bf16[8,2,96,128]{3,2,1,0:T(8,128)(2,1)}, u32[]{:S(2)}) copy-start(bf16[8,2,96,128]{3,2,1,0:T(8,128)(2,1)} %pad_maximum_fusion) | copy-start | bytes 1179652
  436.1 23.0 %collective-permute-start.12 = (f32[8,2,96,64]{2,3,1,0:T(8,128)}, f32[8,2,96,64]{2,3,1,0:T(8,128)}, u32[]{:S(2)}, u32[]{:S(2)}) collective-permute-start(f32[8,2,96,64]{2,3,1,0:T(8,128)} %bitcast_add_fusion.8), channel_id=1, source_target_pairs={{0,2},{2,4},{4,6},{6,0},{1,3},{3,5},{5,7},{7,1},{8,10},{10,12},{12... | collective-permute-start | bytes 1179656 | tf_op jit(solution)/shard_map/ppermute | solution.py:63
Sparse Core Ops, SparseCore 0:
  23.6 82.8 reduce-scatter.2
  113.0 54.7 all-gather.2
  183.8 77.8 reduce-scatter.4
  294.9 55.5 all-gather.4
where the time goes:
time: 473 us; the launch traced here: 471 us
  waiting for transfers between devices  310 us (66%)
  local copies, waits for them, and re-layouts  58.1 us (12%)
  other arithmetic  50.2 us (11%)
  starting transfers between devices  29.8 us (6%)
  between operations  13.4 us (3%)
  matrix products  9.62 us (2%)
    all_gather x2, waiting for transfers between devices, broadcast(): return (lax.all_gather(part, PLANE, axis=0, tiled=True), pending)  110 us
    reduce_scatter x2, waiting for transfers between devices, broadcast(): part = lax.psum_scatter(piece, PLANE, scatter_dimension=0, tiled=True)  83 us
    ppermute x6, waiting for transfers between devices, shot_reduce(): got_b = lax.ppermute(acc_b, 'zh', perm=down)  73.4 us
    ppermute x6, waiting for transfers between devices, shot_reduce(): got_f = lax.ppermute(acc_f, 'zh', perm=up)  27.4 us
    ppermute x6, starting transfers between devices, shot_reduce(): got_b = lax.ppermute(acc_b, 'zh', perm=down)  22 us
    dynamic_slice x6, local copies, waits for them, and re-layouts, shot_reduce(): lax.dynamic_index_in_dim(forward, (zh - 2 - step) % nz, axis=0, keepdims=...  11.7 us
    dynamic_slice x6, local copies, waits for them, and re-layouts, shot_reduce(): lax.dynamic_index_in_dim(backward, (zh + 2 + step) % nz, axis=0, keepdims...  11.7 us
    ppermute x2, waiting for transfers between devices, shot_reduce(): mine = keep + lax.ppermute(send, 'c', perm=[(0, 1), (1, 0)])  10.6 us
  transfers between devices with their start and end apart: 20, of which 17 were waited for; matrix products, arithmetic and copies ran while one was open for 13% of the time, Pallas kernels for 0%

commit v1 on v0

--- a/solution.py
+++ b/solution.py
@@ -39,7 +39,12 @@
     part = part + other
     if pending is not None:
         part, pending = lax.optimization_barrier((part, pending))
-    return (lax.all_gather(part, PLANE, axis=0, tiled=True), pending)
+    return (
+        jnp.concatenate(
+            lax.all_to_all(jnp.stack([part] * lax.axis_size(PLANE)), PLANE, 0, 0), axis=0
+        ),
+        pending,
+    )
 
 
 def shot_reduce(partial):

time: 473 us -> 450 us (0.951)
  the two profiles are of different devices: /device:TPU:1 before, /device:TPU:2 now
where the time goes in v1:
time: 450 us; the launch traced here: 449 us
  waiting for transfers between devices  235 us (52%)
  local copies, waits for them, and re-layouts  63 us (14%)
  other arithmetic  45.2 us (10%)
  blocking collectives  42.4 us (9%)
  starting transfers between devices  40.2 us (9%)
  between operations  13.8 us (3%)
  matrix products  9.62 us (2%)
    reduce_scatter x2, waiting for transfers between devices, broadcast(): part = lax.psum_scatter(piece, PLANE, scatter_dimension=0, tiled=True)  83.6 us
    ppermute x6, waiting for transfers between devices, shot_reduce(): got_b = lax.ppermute(acc_b, 'zh', perm=down)  80.2 us
    all_to_all x1, blocking collectives, broadcast(): lax.all_to_all(jnp.stack([part] * lax.axis_size(PLANE)), PLANE, 0, 0)  42.4 us
    all_to_all x1, waiting for transfers between devices, broadcast(): lax.all_to_all(jnp.stack([part] * lax.axis_size(PLANE)), PLANE, 0, 0)  35.3 us
    ppermute x6, starting transfers between devices, shot_reduce(): got_b = lax.ppermute(acc_b, 'zh', perm=down)  31.8 us
    ppermute x6, waiting for transfers between devices, shot_reduce(): got_f = lax.ppermute(acc_f, 'zh', perm=up)  16.2 us
    dynamic_slice x6, local copies, waits for them, and re-layouts, shot_reduce(): lax.dynamic_index_in_dim(forward, (zh - 2 - step) % nz, axis=0, keepdims=...  11.8 us
    dynamic_slice x6, local copies, waits for them, and re-layouts, shot_reduce(): lax.dynamic_index_in_dim(backward, (zh + 2 + step) % nz, axis=0, keepdims...  11.8 us
  transfers between devices with their start and end apart: 19, of which 15 were waited for; matrix products, arithmetic and copies ran while one was open for 14% of the time, Pallas kernels for 0%

profile of v1, /device:TPU:2, one launch (start us, length us, event | category | flops | bytes accessed | tf_op | source)
XLA Modules:
  0.0 448.8 jit_solution(8970960231975941722)
XLA Ops:
  7.9 3.7 fusion.28
  11.7 3.8 compare_reduce_fusion
  15.6 4.0 convert_bitcast_fusion
  19.6 3.9 slice_bitcast_fusion
  23.5 83.6 %reduce-scatter.3.cloned.1.call-done = bf16[4,2,96,128]{3,2,1,0:T(8,128)(2,1)} async-done(((bf16[64,2,96,128]{3,2,1,0:T(8,128)(2,1)}), bf16[4,2,96,128]{3,2,1,0:T(8,128)(2,1)}) %reduce-scatter.3.cloned.1.call-update) | async-done | bytes 196624 | tf_op jit(solution)/shard_map/reduce_scatter | solution.py:37
  108.6 4.3 collective-permute-done
  114.0 2.3 stack.16
  116.3 5.7 %all-to-all-start = ((bf16[16,4,2,96,128]{4,3,1,2,0:T(8,128)(2,1)}), bf16[16,4,2,96,128]{4,3,1,2,0:T(8,128)(2,1)S(1)}, u32[]{:S(2)}, u32[]{:S(2)}) async-start(bf16[16,4,2,96,128]{4,3,1,2,0:T(8,128)(2,1)} %stack.16), calls=%async_computation.1 | async-start | bytes 6291456 | tf_op jit(solution)/shard_map/all_to_all | solution.py:44
  122.8 35.3 %all-to-all-done = bf16[16,4,2,96,128]{4,3,1,2,0:T(8,128)(2,1)S(1)} async-done(((bf16[16,4,2,96,128]{4,3,1,2,0:T(8,128)(2,1)}), bf16[16,4,2,96,128]{4,3,1,2,0:T(8,128)(2,1)S(1)}, u32[]{:S(2)}, u32[]{:S(2)}) %all-to-all-start) | async-done | bytes 3145760 | tf_op jit(solution)/shard_map/all_to_all | solution.py:44
  162.3 3.6 fusion
  165.9 3.4 broadcast_multiply_fusion.1
  169.6 2.4 copy-done
  172.1 5.7 %collective-permute-done.2 = f32[4,8,2,96,128]{4,3,2,1,0:T(8,128)} collective-permute-done((f32[4,8,2,96,128]{4,3,2,1,0:T(8,128)S(1)}, f32[4,8,2,96,128]{4,3,2,1,0:T(8,128)}, u32[]{:S(2)}, u32[]{:S(2)}) %collective-permute-start.2) | collective-permute-done | bytes 3145760 | tf_op jit(solution)/shard_map/ppermute | solution.py:59
  177.8 3.4 bitcast_add_fusion.1
  187.7 4.1 collective-permute-start.6
  199.9 20.6 %collective-permute-done.6 = f32[8,2,96,64]{2,3,1,0:T(8,128)} collective-permute-done((f32[8,2,96,64]{2,3,1,0:T(8,128)}, f32[8,2,96,64]{2,3,1,0:T(8,128)}, u32[]{:S(2)}, u32[]{:S(2)}) %collective-permute-start.6) | collective-permute-done | bytes 393248 | tf_op jit(solution)/shard_map/ppermute | solution.py:69
  222.5 4.7 %collective-permute-start.7 = (f32[8,2,96,64]{2,3,1,0:T(8,128)}, f32[8,2,96,64]{2,3,1,0:T(8,128)}, u32[]{:S(2)}, u32[]{:S(2)}) collective-permute-start(f32[8,2,96,64]{2,3,1,0:T(8,128)} %bitcast_add_fusion.11), channel_id=1, source_target_pairs={{0,6},{2,0},{4,2},{6,4},{1,7},{3,1},{5,3},{7,5},{8,14},{10,8},{12,... | collective-permute-start | bytes 1179656 | tf_op jit(solution)/shard_map/ppermute | solution.py:69
  233.7 6.4 %collective-permute-done.7 = f32[8,2,96,64]{2,3,1,0:T(8,128)} collective-permute-done((f32[8,2,96,64]{2,3,1,0:T(8,128)}, f32[8,2,96,64]{2,3,1,0:T(8,128)}, u32[]{:S(2)}, u32[]{:S(2)}) %collective-permute-start.7) | collective-permute-done | bytes 393248 | tf_op jit(solution)/shard_map/ppermute | solution.py:69
  242.1 10.4 %collective-permute-start.8 = (f32[8,2,96,64]{2,3,1,0:T(8,128)}, f32[8,2,96,64]{2,3,1,0:T(8,128)}, u32[]{:S(2)}, u32[]{:S(2)}) collective-permute-start(f32[8,2,96,64]{2,3,1,0:T(8,128)} %bitcast_add_fusion.10), channel_id=1, source_target_pairs={{0,6},{2,0},{4,2},{6,4},{1,7},{3,1},{5,3},{7,5},{8,14},{10,8},{12,... | collective-permute-start | bytes 1179656 | tf_op jit(solution)/shard_map/ppermute | solution.py:69
  255.2 9.0 %collective-permute-done.8 = f32[8,2,96,64]{2,3,1,0:T(8,128)} collective-permute-done((f32[8,2,96,64]{2,3,1,0:T(8,128)}, f32[8,2,96,64]{2,3,1,0:T(8,128)}, u32[]{:S(2)}, u32[]{:S(2)}) %collective-permute-start.8) | collective-permute-done | bytes 393248 | tf_op jit(solution)/shard_map/ppermute | solution.py:69
  266.4 9.8 %collective-permute-done.5 = f32[8,2,96,64]{2,3,1,0:T(8,128)} collective-permute-done((f32[8,2,96,64]{2,3,1,0:T(8,128)}, f32[8,2,96,64]{2,3,1,0:T(8,128)}, u32[]{:S(2)}, u32[]{:S(2)}) %collective-permute-start.5) | collective-permute-done | bytes 393248 | tf_op jit(solution)/shard_map/ppermute | solution.py:68
  282.2 3.6 collective-permute-done.1
  286.7 42.4 %all_to_all.10 = bf16[16,4,2,96,128]{4,3,1,2,0:T(8,128)(2,1)S(1)} all-to-all(bf16[16,4,2,96,128]{4,3,1,2,0:T(8,128)(2,1)S(1)} %stack.20), channel_id=1, replica_groups=mesh['y'=4,'x'=4,'zl'=2,'zh'=4,'c'=2] {'y','x'}, dimensions={0} | all-to-all | bytes 6291456 | tf_op jit(solution)/shard_map/all_to_all | solution.py:44
  335.7 5.6 %collective-permute-done.9 = f32[4,8,2,96,128]{4,3,2,1,0:T(8,128)S(1)} collective-permute-done((f32[4,8,2,96,128]{4,3,2,1,0:T(8,128)S(1)}, f32[4,8,2,96,128]{4,3,2,1,0:T(8,128)S(1)}, u32[]{:S(2)}, u32[]{:S(2)}) %collective-permute-start.9) | collective-permute-done | bytes 3145760 | tf_op jit(solution)/shard_map/ppermute | solution.py:59
  348.4 4.3 collective-permute-start.13
  358.6 15.8 %collective-permute-done.13 = f32[8,2,96,64]{2,3,1,0:T(8,128)} collective-permute-done((f32[8,2,96,64]{2,3,1,0:T(8,128)}, f32[8,2,96,64]{2,3,1,0:T(8,128)}, u32[]{:S(2)}, u32[]{:S(2)}) %collective-permute-start.13) | collective-permute-done | bytes 393248 | tf_op jit(solution)/shard_map/ppermute | solution.py:69
  376.5 3.7 collective-permute-start.14
  389.0 14.2 %collective-permute-done.14 = f32[8,2,96,64]{2,3,1,0:T(8,128)} collective-permute-done((f32[8,2,96,64]{2,3,1,0:T(8,128)}, f32[8,2,96,64]{2,3,1,0:T(8,128)}, u32[]{:S(2)}, u32[]{:S(2)}) %collective-permute-start.14) | collective-permute-done | bytes 393248 | tf_op jit(solution)/shard_map/ppermute | solution.py:69
  404.4 4.7 %collective-permute-start.15 = (f32[8,2,96,64]{2,3,1,0:T(8,128)S(1)}, f32[8,2,96,64]{2,3,1,0:T(8,128)}, u32[]{:S(2)}, u32[]{:S(2)}) collective-permute-start(f32[8,2,96,64]{2,3,1,0:T(8,128)S(1)} %bitcast_add_fusion.6), channel_id=1, source_target_pairs={{0,6},{2,0},{4,2},{6,4},{1,7},{3,1},{5,3},{7,5},{8,14},{10,8},{12,... | collective-permute-start | bytes 1179656 | tf_op jit(solution)/shard_map/ppermute | solution.py:69
  409.1 2.5 collective-permute-done.11
  413.6 14.4 %collective-permute-done.15 = f32[8,2,96,64]{2,3,1,0:T(8,128)} collective-permute-done((f32[8,2,96,64]{2,3,1,0:T(8,128)S(1)}, f32[8,2,96,64]{2,3,1,0:T(8,128)}, u32[]{:S(2)}, u32[]{:S(2)}) %collective-permute-start.15) | collective-permute-done | bytes 393248 | tf_op jit(solution)/shard_map/ppermute | solution.py:69
  432.4 3.9 collective-permute-done.12
  (96 shorter events, 89.9 us)
Async XLA Ops:
  6.5 100.5 %reduce-scatter.3.cloned.1.call-start = ((), (), s32[]{:S(2)}) async-start(), calls=%async_computation.4 | async-start | bytes 3342336 | tf_op jit(solution)/shard_map/reduce_scatter | solution.py:37
  107.1 5.9 %collective-permute-start = (bf16[4,2,96,128]{3,2,1,0:T(8,128)(2,1)}, bf16[4,2,96,128]{3,2,1,0:T(8,128)(2,1)S(1)}, u32[]{:S(2)}, u32[]{:S(2)}) collective-permute-start(bf16[4,2,96,128]{3,2,1,0:T(8,128)(2,1)} %reduce-scatter.3.cloned.1.call-done), channel_id=1, source_target_pairs={{0,8},{8,0},{1,9},{9,1},{2,10},{10,2},{3,11},{11,3},{4,12},{12,4},... | collective-permute-start | bytes 589832 | tf_op jit(solution)/shard_map/ppermute | solution.py:38
  116.3 41.8 %all-to-all-start = ((bf16[16,4,2,96,128]{4,3,1,2,0:T(8,128)(2,1)}), bf16[16,4,2,96,128]{4,3,1,2,0:T(8,128)(2,1)S(1)}, u32[]{:S(2)}, u32[]{:S(2)}) async-start(bf16[16,4,2,96,128]{4,3,1,2,0:T(8,128)(2,1)} %stack.16), calls=%async_computation.1 | async-start | bytes 6291456 | tf_op jit(solution)/shard_map/all_to_all | solution.py:44
  122.0 157.9 %reduce-scatter.5.cloned.1.call-start = ((), (), s32[]{:S(2)}) async-start(), calls=%async_computation.5 | async-start | bytes 3342336 | tf_op jit(solution)/shard_map/reduce_scatter | solution.py:37
  160.1 2.2 copy-start.3
  169.4 2.6 copy-start
  172.0 5.8 %collective-permute-start.2 = (f32[4,8,2,96,128]{4,3,2,1,0:T(8,128)S(1)}, f32[4,8,2,96,128]{4,3,2,1,0:T(8,128)}, u32[]{:S(2)}, u32[]{:S(2)}) collective-permute-start(f32[4,8,2,96,128]{4,3,2,1,0:T(8,128)S(1)} %dynamic-slice_bitcast_fusion.1), channel_id=1, source_target_pairs={{0,1},{1,0},{2,3},{3,2},{4,5},{5,4},{6,7},{7,6},{8,9},{9,8},{10,11... | collective-permute-start | bytes 9437192 | tf_op jit(solution)/shard_map/ppermute | solution.py:59
  182.4 1.6 copy-start.1
  187.7 32.8 %collective-permute-start.6 = (f32[8,2,96,64]{2,3,1,0:T(8,128)}, f32[8,2,96,64]{2,3,1,0:T(8,128)}, u32[]{:S(2)}, u32[]{:S(2)}) collective-permute-start(f32[8,2,96,64]{2,3,1,0:T(8,128)} %bitcast.117), channel_id=1, source_target_pairs={{0,6},{2,0},{4,2},{6,4},{1,7},{3,1},{5,3},{7,5},{8,14},{10,8},{12,... | collective-permute-start | bytes 1179656 | tf_op jit(solution)/shard_map/ppermute | solution.py:69
  195.5 31.7 %collective-permute-start.3 = (f32[8,2,96,64]{2,3,1,0:T(8,128)}, f32[8,2,96,64]{2,3,1,0:T(8,128)}, u32[]{:S(2)}, u32[]{:S(2)}) collective-permute-start(f32[8,2,96,64]{2,3,1,0:T(8,128)} %bitcast.119), channel_id=1, source_target_pairs={{0,2},{2,4},{4,6},{6,0},{1,3},{3,5},{5,7},{7,1},{8,10},{10,12},{12... | collective-permute-start | bytes 1179656 | tf_op jit(solution)/shard_map/ppermute | solution.py:68
  222.5 17.5 %collective-permute-start.7 = (f32[8,2,96,64]{2,3,1,0:T(8,128)}, f32[8,2,96,64]{2,3,1,0:T(8,128)}, u32[]{:S(2)}, u32[]{:S(2)}) collective-permute-start(f32[8,2,96,64]{2,3,1,0:T(8,128)} %bitcast_add_fusion.11), channel_id=1, source_target_pairs={{0,6},{2,0},{4,2},{6,4},{1,7},{3,1},{5,3},{7,5},{8,14},{10,8},{12,... | collective-permute-start | bytes 1179656 | tf_op jit(solution)/shard_map/ppermute | solution.py:69
  229.2 23.3 %collective-permute-start.4 = (f32[8,2,96,64]{2,3,1,0:T(8,128)}, f32[8,2,96,64]{2,3,1,0:T(8,128)}, u32[]{:S(2)}, u32[]{:S(2)}) collective-permute-start(f32[8,2,96,64]{2,3,1,0:T(8,128)} %bitcast_add_fusion.13), channel_id=1, source_target_pairs={{0,2},{2,4},{4,6},{6,0},{1,3},{3,5},{5,7},{7,1},{8,10},{10,12},{12... | collective-permute-start | bytes 1179656 | tf_op jit(solution)/shard_map/ppermute | solution.py:68
  242.1 22.1 %collective-permute-start.8 = (f32[8,2,96,64]{2,3,1,0:T(8,128)}, f32[8,2,96,64]{2,3,1,0:T(8,128)}, u32[]{:S(2)}, u32[]{:S(2)}) collective-permute-start(f32[8,2,96,64]{2,3,1,0:T(8,128)} %bitcast_add_fusion.10), channel_id=1, source_target_pairs={{0,6},{2,0},{4,2},{6,4},{1,7},{3,1},{5,3},{7,5},{8,14},{10,8},{12,... | collective-permute-start | bytes 1179656 | tf_op jit(solution)/shard_map/ppermute | solution.py:69
  254.6 21.6 %collective-permute-start.5 = (f32[8,2,96,64]{2,3,1,0:T(8,128)}, f32[8,2,96,64]{2,3,1,0:T(8,128)}, u32[]{:S(2)}, u32[]{:S(2)}) collective-permute-start(f32[8,2,96,64]{2,3,1,0:T(8,128)} %bitcast_add_fusion.12), channel_id=1, source_target_pairs={{0,2},{2,4},{4,6},{6,0},{1,3},{3,5},{5,7},{7,1},{8,10},{10,12},{12... | collective-permute-start | bytes 1179656 | tf_op jit(solution)/shard_map/ppermute | solution.py:68
  279.9 6.0 %copy-start.6 = (bf16[4,2,96,128]{3,2,1,0:T(8,128)(2,1)S(1)}, bf16[4,2,96,128]{3,2,1,0:T(8,128)(2,1)}, u32[]{:S(2)}) copy-start(bf16[4,2,96,128]{3,2,1,0:T(8,128)(2,1)} %reduce-scatter.5.cloned.1.call-done) | copy-start | bytes 589828
  279.9 6.0 %collective-permute-start.1 = (bf16[4,2,96,128]{3,2,1,0:T(8,128)(2,1)}, bf16[4,2,96,128]{3,2,1,0:T(8,128)(2,1)S(1)}, u32[]{:S(2)}, u32[]{:S(2)}) collective-permute-start(bf16[4,2,96,128]{3,2,1,0:T(8,128)(2,1)} %reduce-scatter.5.cloned.1.call-done), channel_id=1, source_target_pairs={{0,8},{8,0},{1,9},{9,1},{2,10},{10,2},{3,11},{11,3},{4,12},{12,4},... | collective-permute-start | bytes 589832 | tf_op jit(solution)/shard_map/ppermute | solution.py:38
  331.0 2.2 copy-start.4
  335.4 6.0 %collective-permute-start.9 = (f32[4,8,2,96,128]{4,3,2,1,0:T(8,128)S(1)}, f32[4,8,2,96,128]{4,3,2,1,0:T(8,128)S(1)}, u32[]{:S(2)}, u32[]{:S(2)}) collective-permute-start(f32[4,8,2,96,128]{4,3,2,1,0:T(8,128)S(1)} %dynamic-slice_bitcast_fusion), channel_id=1, source_target_pairs={{0,1},{1,0},{2,3},{3,2},{4,5},{5,4},{6,7},{7,6},{8,9},{9,8},{10,11... | collective-permute-start | bytes 9437192 | tf_op jit(solution)/shard_map/ppermute | solution.py:59
  343.1 1.6 copy-start.2
  348.4 25.9 %collective-permute-start.13 = (f32[8,2,96,64]{2,3,1,0:T(8,128)}, f32[8,2,96,64]{2,3,1,0:T(8,128)}, u32[]{:S(2)}, u32[]{:S(2)}) collective-permute-start(f32[8,2,96,64]{2,3,1,0:T(8,128)} %bitcast.118), channel_id=1, source_target_pairs={{0,6},{2,0},{4,2},{6,4},{1,7},{3,1},{5,3},{7,5},{8,14},{10,8},{12,... | collective-permute-start | bytes 1179656 | tf_op jit(solution)/shard_map/ppermute | solution.py:69
  356.4 26.0 %collective-permute-start.10 = (f32[8,2,96,64]{2,3,1,0:T(8,128)}, f32[8,2,96,64]{2,3,1,0:T(8,128)}, u32[]{:S(2)}, u32[]{:S(2)}) collective-permute-start(f32[8,2,96,64]{2,3,1,0:T(8,128)} %bitcast.120), channel_id=1, source_target_pairs={{0,2},{2,4},{4,6},{6,0},{1,3},{3,5},{5,7},{7,1},{8,10},{10,12},{12... | collective-permute-start | bytes 1179656 | tf_op jit(solution)/shard_map/ppermute | solution.py:68
  376.5 26.7 %collective-permute-start.14 = (f32[8,2,96,64]{2,3,1,0:T(8,128)}, f32[8,2,96,64]{2,3,1,0:T(8,128)}, u32[]{:S(2)}, u32[]{:S(2)}) collective-permute-start(f32[8,2,96,64]{2,3,1,0:T(8,128)} %bitcast_add_fusion.7), channel_id=1, source_target_pairs={{0,6},{2,0},{4,2},{6,4},{1,7},{3,1},{5,3},{7,5},{8,14},{10,8},{12,... | collective-permute-start | bytes 1179656 | tf_op jit(solution)/shard_map/ppermute | solution.py:69
  384.5 27.1 %collective-permute-start.11 = (f32[8,2,96,64]{2,3,1,0:T(8,128)}, f32[8,2,96,64]{2,3,1,0:T(8,128)}, u32[]{:S(2)}, u32[]{:S(2)}) collective-permute-start(f32[8,2,96,64]{2,3,1,0:T(8,128)} %bitcast_add_fusion.9), channel_id=1, source_target_pairs={{0,2},{2,4},{4,6},{6,0},{1,3},{3,5},{5,7},{7,1},{8,10},{10,12},{12... | collective-permute-start | bytes 1179656 | tf_op jit(solution)/shard_map/ppermute | solution.py:68
  404.4 23.6 %collective-permute-start.15 = (f32[8,2,96,64]{2,3,1,0:T(8,128)S(1)}, f32[8,2,96,64]{2,3,1,0:T(8,128)}, u32[]{:S(2)}, u32[]{:S(2)}) collective-permute-start(f32[8,2,96,64]{2,3,1,0:T(8,128)S(1)} %bitcast_add_fusion.6), channel_id=1, source_target_pairs={{0,6},{2,0},{4,2},{6,4},{1,7},{3,1},{5,3},{7,5},{8,14},{10,8},{12,... | collective-permute-start | bytes 1179656 | tf_op jit(solution)/shard_map/ppermute | solution.py:69
  413.6 26.1 %copy-start.5 = (bf16[8,2,96,128]{3,2,1,0:T(8,128)(2,1)S(1)}, bf16[8,2,96,128]{3,2,1,0:T(8,128)(2,1)}, u32[]{:S(2)}) copy-start(bf16[8,2,96,128]{3,2,1,0:T(8,128)(2,1)} %pad_maximum_fusion) | copy-start | bytes 1179652
  413.6 22.6 %collective-permute-start.12 = (f32[8,2,96,64]{2,3,1,0:T(8,128)}, f32[8,2,96,64]{2,3,1,0:T(8,128)}, u32[]{:S(2)}, u32[]{:S(2)}) collective-permute-start(f32[8,2,96,64]{2,3,1,0:T(8,128)} %bitcast_add_fusion.8), channel_id=1, source_target_pairs={{0,2},{2,4},{4,6},{6,0},{1,3},{3,5},{5,7},{7,1},{8,10},{10,12},{12... | collective-permute-start | bytes 1179656 | tf_op jit(solution)/shard_map/ppermute | solution.py:68
Sparse Core Ops, SparseCore 0:
  23.6 83.4 reduce-scatter.2
  172.2 81.7 reduce-scatter.4
